TPU v7x, 32 devices: a whole 2x2x4 slice. The times are simulated.
32 devices in a mesh: tok: 8 (over z, x), grp: 4 (over y, core).
Axes of the slice: x: 2, y: 2, z: 4, core: 2. Of those that a mesh axis runs over, the one named last changes fastest.
Arguments:
- queries: bfloat16 [1536, 2048], P('tok', 'grp'), may hold values from -72 to 72
- new_keys: bfloat16 [1536, 2048], P('tok', 'grp'), may hold values from -8 to 8
- new_values: bfloat16 [1536, 2048], P('tok', 'grp'), may hold values from -6 to 6
- residual: bfloat16 [1536, 2048], P('tok', 'grp'), may hold values from -6 to 6
- w_out: bfloat16 [2048, 2048], P('grp'), may hold values from -0.125 to 0.125
- leaf_keys: bfloat16 [8, 512, 2048], P('tok', None, 'grp'), may hold values from -6 to 6
- leaf_values: bfloat16 [8, 512, 2048], P('tok', None, 'grp'), may hold values from -6 to 6
- upper_keys: bfloat16 [6, 1024, 2048], P(None, 'tok', 'grp'), may hold values from -8 to 8
- upper_values: bfloat16 [6, 1024, 2048], P(None, 'tok', 'grp'), may hold values from -6 to 6
- req_len: int32 [8], replicated, may hold values from 48 to 192, as said below
- leaf_mid: int32 [8], replicated, may hold values from 0 to 3
- mid_root: int32 [4], replicated, may hold values from 0 to 1, as said below
- upper_len: int32 [6], replicated, may hold values from 256 to 1024, as said below
- leaf_len: int32 [8], replicated, may hold values from 128 to 512, as said below
Outputs:
- hidden_out: bfloat16 [1536, 2048], P('tok', 'grp')
Inputs may be any that keep to these rules, and one draw needn't show every extreme that they name: `req_len`: some request has exactly 192 new tokens. `mid_root`: each root is the parent of 2 mids. `upper_len`: the first 2 entries are roots and equal 1024. `leaf_len`: some leaf has exactly 512 positions.
All inputs are finite; a program needn't handle non-finite values.
Results may differ from a plain program's by a relative error of at most 0.008.
Values may be sent and summed in bfloat16 or wider, within the bound.
No kernel may reach another device: no remote copies, remote signals or barrier semaphores. Data moves between devices by JAX's collectives and lax.ppermute only.
A program may use at most 64 MiB of HBM per device.

v0:
```python
import math
import jax
import jax.numpy as jnp
from jax import lax
from jax.sharding import PartitionSpec as P

HEAD_DIM = 128
NEG_FILL = -1e30


def partial_attention(query_rows, key_rows, values, allowed, head_count):
    head_width = query_rows.shape[1] // head_count
    query_heads = query_rows.reshape(query_rows.shape[0], head_count, head_width)
    key_heads = key_rows.reshape(key_rows.shape[0], head_count, head_width)
    value_heads = values.reshape(values.shape[0], head_count, head_width)
    scores = jnp.einsum(
        "qhd,khd->hqk", query_heads, key_heads, preferred_element_type=jnp.float32
    ) * head_width ** (-0.5)
    scores = jnp.where(allowed[None], scores, NEG_FILL)
    row_max = jnp.max(scores, axis=2)
    exp_scores = jnp.where(allowed[None], jnp.exp(scores - row_max[:, :, None]), 0.0)
    row_total = jnp.sum(exp_scores, axis=2)
    weighted = jnp.einsum(
        "hqk,khd->hqd",
        exp_scores.astype(jnp.bfloat16),
        value_heads,
        preferred_element_type=jnp.float32,
    )
    return (row_max, row_total, weighted)


def combine(earlier, latter):
    new_max = jnp.maximum(earlier[0], latter[0])
    earlier_scale = jnp.exp(earlier[0] - new_max)
    latter_scale = jnp.exp(latter[0] - new_max)
    return (
        new_max,
        earlier[1] * earlier_scale + latter[1] * latter_scale,
        earlier[2] * earlier_scale[:, :, None] + latter[2] * latter_scale[:, :, None],
    )


def node_attention(carry, query_rows, node_keys, node_values, node_len, head_count):
    node_rows = node_keys.shape[0]
    block = math.gcd(node_rows, 512)
    row_count = query_rows.shape[0]
    for start in range(0, node_rows, block):
        positions = start + jnp.arange(block, dtype=jnp.int32)
        allowed = jnp.broadcast_to((positions < node_len)[None, :], (row_count, block))
        piece_part = partial_attention(
            query_rows,
            node_keys[start : start + block],
            node_values[start : start + block],
            allowed,
            head_count,
        )
        carry = combine(carry, piece_part)
    return carry


def shards(
    queries,
    new_keys,
    new_values,
    residual,
    w_out,
    leaf_keys,
    leaf_values,
    upper_keys,
    upper_values,
    req_len,
    leaf_mid,
    mid_root,
    upper_len,
    leaf_len,
):
    dev_count = lax.axis_size("tok")
    my_index = lax.axis_index("tok")
    row_count = queries.shape[0]
    col_count = queries.shape[1]
    head_count = col_count // HEAD_DIM
    mid_count = mid_root.shape[0]
    node_count = upper_len.shape[0]
    root_count = node_count - mid_count
    owned = (jnp.arange(dev_count, dtype=jnp.int32) == my_index).astype(jnp.int32)
    my_length = jnp.sum(owned * req_len)
    my_mid = jnp.sum(owned * leaf_mid)
    my_leaf_len = jnp.sum(owned * leaf_len)
    my_root = jnp.sum((jnp.arange(mid_count) == my_mid).astype(jnp.int32) * mid_root)
    node_ids = jnp.arange(node_count)
    root_len = jnp.sum((node_ids == my_root).astype(jnp.int32) * upper_len)
    mid_len = jnp.sum((node_ids == root_count + my_mid).astype(jnp.int32) * upper_len)
    position = jnp.arange(row_count, dtype=jnp.int32)
    is_live = position < my_length
    leaf_count = leaf_keys.shape[1]
    local_keys = jnp.concatenate([leaf_keys[0], new_keys], axis=0)
    local_values = jnp.concatenate([leaf_values[0], new_values], axis=0)
    leaf_allowed = jnp.broadcast_to(
        (jnp.arange(leaf_count) < my_leaf_len)[None, :], (row_count, leaf_count)
    )
    new_allowed = (position[None, :] <= position[:, None]) & is_live[None, :]
    local_part = partial_attention(
        queries,
        local_keys,
        local_values,
        jnp.concatenate([leaf_allowed, new_allowed], axis=1),
        head_count,
    )
    gathered_keys, gathered_values = (
        lax.all_gather(upper_keys, "tok", axis=1, tiled=True),
        lax.all_gather(upper_values, "tok", axis=1, tiled=True),
    )
    merged = node_attention(
        local_part, queries, gathered_keys[my_root], gathered_values[my_root], root_len, head_count
    )
    merged = node_attention(
        merged,
        queries,
        gathered_keys[root_count + my_mid],
        gathered_values[root_count + my_mid],
        mid_len,
        head_count,
    )
    attended = (merged[2] / merged[1][:, :, None]).transpose(1, 0, 2).reshape(row_count, col_count)
    attention = jnp.where(is_live[:, None], attended, 0.0).astype(jnp.bfloat16)
    projected = jnp.dot(attention, w_out, preferred_element_type=jnp.float32)
    mixed = lax.psum_scatter(
        projected.astype(jnp.bfloat16), "grp", scatter_dimension=1, tiled=True
    ).astype(jnp.float32)
    return (residual.astype(jnp.float32) + mixed).astype(jnp.bfloat16)


def solution(mesh):
    in_specs = (
        P("tok", "grp"),
        P("tok", "grp"),
        P("tok", "grp"),
        P("tok", "grp"),
        P("grp", None),
        P("tok", None, "grp"),
        P("tok", None, "grp"),
        P(None, "tok", "grp"),
        P(None, "tok", "grp"),
        P(),
        P(),
        P(),
        P(),
        P(),
    )
    out_specs = P("tok", "grp")
    return jax.shard_map(shards, mesh=mesh, in_specs=in_specs, out_specs=out_specs, check_vma=False)
```

profile of v0, /device:TPU:0, one launch (start us, length us, event | category | flops | bytes accessed | tf_op | source)
XLA Modules:
  0.0 251.3 jit_solution(10677370438847150841)
XLA Ops:
  6.5 2.5 copy.27
  9.1 1.2 copy.30
  12.3 1.3 fusion.91
  15.1 1.0 copy.21
  16.2 1.3 copy.24
  18.9 1.2 fusion.92
  21.4 0.7 fusion.90
  22.0 0.7 iota_compare_fusion.2
  23.3 0.6 iota_compare_fusion.4
  24.1 1.0 copy_bitcast_fusion
  25.1 1.7 fusion
  26.9 1.4 copy-done.10
  28.3 0.9 fusion.1
  29.1 82.9 %all-gather.3.cloned.1.call-done = bf16[6,1024,512]{1,2,0:T(8,128)(2,1)} async-done(((bf16[6,128,512]{1,2,0:T(8,128)(2,1)}), bf16[6,1024,512]{1,2,0:T(8,128)(2,1)}) %all-gather.3.cloned.1.call-update) | async-done | bytes 6291472 | tf_op jit(solution)/shard_map/all_gather | solution.py:110
  112.1 1.7 constant_dynamic-slice_fusion.3
  117.7 1.1 copy-done.7
  119.4 92.8 %all-gather.5.cloned.1.call-done = bf16[6,1024,512]{1,2,0:T(8,128)(2,1)} async-done(((bf16[6,128,512]{1,2,0:T(8,128)(2,1)}), bf16[6,1024,512]{1,2,0:T(8,128)(2,1)}) %all-gather.5.cloned.1.call-update) | async-done | bytes 6291472 | tf_op jit(solution)/shard_map/all_gather | solution.py:111
  212.3 1.8 constant_dynamic-slice_fusion.4
  214.8 0.7 copy-done.8
  216.6 1.0 fusion.31
  218.5 0.8 copy-done.4
  219.9 1.5 convolution_convert_fusion
  221.4 21.6 %reduce-scatter.2.cloned.1.call-done = bf16[192,512]{1,0:T(8,128)(2,1)} async-done(((bf16[192,2048]{1,0:T(8,128)(2,1)}), bf16[192,512]{1,0:T(8,128)(2,1)}) %reduce-scatter.2.cloned.1.call-update) | async-done | bytes 196624 | tf_op jit(solution)/shard_map/reduce_scatter | solution.py:127
  243.1 1.7 add_convert_fusion
  (68 shorter events, 11.6 us)
Async XLA Ops:
  6.5 213.3 %copy-start = (bf16[512,2048]{1,0:T(8,128)(2,1)S(1)}, bf16[512,2048]{1,0:T(8,128)(2,1)}, u32[]{:S(2)}) copy-start(bf16[512,2048]{1,0:T(8,128)(2,1)} %param.18) | copy-start | bytes 6291460
  6.5 2.6 %copy-start.12 = (bf16[6,128,512]{2,1,0:T(8,128)(2,1)S(1)}, bf16[6,128,512]{2,1,0:T(8,128)(2,1)}, u32[]{:S(2)}) copy-start(bf16[6,128,512]{2,1,0:T(8,128)(2,1)} %param.22) | copy-start | bytes 2359300
  6.5 105.5 %all-gather.3.cloned.1.call-start = ((), (), s32[]{:S(2)}) async-start(), calls=%async_computation.1 | async-start | bytes 7077888 | tf_op jit(solution)/shard_map/all_gather | solution.py:110
  9.0 1.3 copy-start.16
  9.0 1.4 copy-start.17
  9.0 3.3 %copy-start.19 = (s32[4]{0:T(128)S(1)}, s32[4]{0:T(128)}, u32[]{:S(2)}) copy-start(s32[4]{0:T(128)} %param.25) | copy-start | bytes 52
  9.0 5.8 %copy-start.13 = (bf16[1,512,512]{2,1,0:T(8,128)(2,1)S(1)}, bf16[1,512,512]{2,1,0:T(8,128)(2,1)}, u32[]{:S(2)}) copy-start(bf16[1,512,512]{2,1,0:T(8,128)(2,1)} %param.19) | copy-start | bytes 1572868
  9.0 203.2 %all-gather.5.cloned.1.call-start = ((), (), s32[]{:S(2)}) async-start(), calls=%async_computation.2 | async-start | bytes 7077888 | tf_op jit(solution)/shard_map/all_gather | solution.py:111
  10.3 232.8 %reduce-scatter.2.cloned.1.call-start = ((), (), s32[]{:S(2)}) async-start(), calls=%async_computation.3 | async-start | bytes 983040 | tf_op jit(solution)/shard_map/reduce_scatter | solution.py:127
  15.1 3.9 %copy-start.18 = (s32[6]{0:T(128)S(1)}, s32[6]{0:T(128)}, u32[]{:S(2)}) copy-start(s32[6]{0:T(128)} %param.26) | copy-start | bytes 76
  15.1 7.6 %copy-start.20 = (s32[8]{0:T(128)S(1)}, s32[8]{0:T(128)}, u32[]{:S(2)}) copy-start(s32[8]{0:T(128)} %param.23) | copy-start | bytes 100
  15.1 9.0 %copy-start.14 = (bf16[192,512]{1,0:T(8,128)(2,1)S(1)}, bf16[192,512]{1,0:T(8,128)(2,1)}, u32[]{:S(2)}) copy-start(bf16[192,512]{1,0:T(8,128)(2,1)} %param.15) | copy-start | bytes 589828
  16.2 8.9 %copy-start.9 = (bf16[192,512]{1,0:T(8,128)(2,1)S(1)}, bf16[192,512]{1,0:T(8,128)(2,1)}, u32[]{:S(2)}) copy-start(bf16[192,512]{1,0:T(8,128)(2,1)} %param.14) | copy-start | bytes 589828
  26.8 1.4 copy-start.10
  114.2 1.2 copy-start.3
  115.3 1.2 copy-start.5
  116.5 1.2 copy-start.1
  117.7 1.1 copy-start.7
  212.3 2.0 copy-start.6
  214.0 1.5 copy-start.8
  214.8 1.8 copy-start.11
  216.6 1.4 copy-start.2
  218.0 1.4 copy-start.4
  219.9 23.2 %copy-start.15 = (bf16[192,512]{1,0:T(8,128)(2,1)S(1)}, bf16[192,512]{1,0:T(8,128)(2,1)}, u32[]{:S(2)}) copy-start(bf16[192,512]{1,0:T(8,128)(2,1)} %param.17) | copy-start | bytes 589828
Sparse Core Ops, SparseCore 0:
  9.4 102.6 all-gather.2
  114.1 98.1 all-gather.4
  221.6 21.4 reduce-scatter.1
where the time goes:
time: 252 us; the launch traced here: 251 us
  waiting for transfers between devices  197 us (78%)
  local copies, waits for them, and re-layouts  16.9 us (7%)
  between operations  16.5 us (7%)
  other arithmetic  12.3 us (5%)
  matrix products  8.03 us (3%)
    all_gather x1, waiting for transfers between devices, shards(): lax.all_gather(upper_values, 'tok', axis=1, tiled=True)  92.8 us
    all_gather x1, waiting for transfers between devices, shards(): lax.all_gather(upper_keys, 'tok', axis=1, tiled=True)  82.9 us
    reduce_scatter x1, waiting for transfers between devices, shards(): lax.psum_scatter(projected.astype(jnp.bfloat16), 'grp', scatter_dimension...  21.6 us
    unnamed x46, local copies, waits for them, and re-layouts  11.2 us
  transfers between devices with their start and end apart: 3, of which 3 were waited for; matrix products, arithmetic and copies ran while one was open for 8% of the time, Pallas kernels for 0%

commit v1 on v0

--- a/solution.py
+++ b/solution.py
@@ -1,3 +1,4 @@
+import functools
 import math
 import jax
 import jax.numpy as jnp
@@ -6,6 +7,36 @@
 
 HEAD_DIM = 128
 NEG_FILL = -1e30
+
+
+def waves_cut(panel, device_axis):
+    extra = lax.axis_size(device_axis)
+    oldest = lax.axis_index(device_axis)
+    block_now, reached, u_next = (extra, oldest, panel.shape[1])
+    row_list = []
+    for num in range(block_now):
+        row_list.append((num, (num + 1) % block_now))
+    items = []
+    for num in range(block_now):
+        items.append((num, (num - 1) % block_now))
+    plain = jnp.zeros((*panel.shape[:1], block_now * u_next, *panel.shape[2:]), panel.dtype)
+    plain = lax.dynamic_update_slice_in_dim(plain, panel, reached * u_next, axis=1)
+    view_out = vec_out = panel
+    back = block_now // 2
+    for ii in range(1, back + 1):
+        view_out = lax.ppermute(view_out, axis_name=device_axis, perm=row_list)
+        plain = lax.dynamic_update_slice_in_dim(
+            plain, view_out, (reached - ii) % block_now * u_next, axis=1
+        )
+        if ii < block_now - back:
+            vec_out = lax.ppermute(vec_out, axis_name=device_axis, perm=items)
+            plain = lax.dynamic_update_slice_in_dim(
+                plain, vec_out, (reached + ii) % block_now * u_next, axis=1
+            )
+    return plain
+
+
+drive_table = functools.partial(waves_cut, device_axis="tok")
 
 
 def partial_attention(query_rows, key_rows, values, allowed, head_count):
@@ -107,7 +138,7 @@
         head_count,
     )
     gathered_keys, gathered_values = (
-        lax.all_gather(upper_keys, "tok", axis=1, tiled=True),
+        drive_table(upper_keys),
         lax.all_gather(upper_values, "tok", axis=1, tiled=True),
     )
     merged = node_attention(

time: 252 us -> 240 us (0.952)
  waiting for transfers between devices: 197 us -> 158 us
  starting transfers between devices: 0.09 us -> 19.8 us
  local copies, waits for them, and re-layouts: 16.9 us -> 23.5 us
    ppermute x0 -> x7, waiting for transfers between devices: none -> 118 us  [the longest x4 105 us: waves_cut(): view_out = lax.ppermute(view_out, axis_name=device_axis, perm=row_list)]
    all_gather x1 -> x0, waiting for transfers between devices: 82.9 us -> none  [shards(): lax.all_gather(upper_keys, 'tok', axis=1, tiled=True)]
    all_gather x1, waiting for transfers between devices: 92.8 us -> 17.3 us  [shards(): lax.all_gather(upper_values, 'tok', axis=1, tiled=True)]
    ppermute x0 -> x7, starting transfers between devices: none -> 19.7 us  [the longest x4 10.4 us: waves_cut(): view_out = lax.ppermute(view_out, axis_name=device_axis, perm=row_list)]
    dynamic_update_slice x0 -> x8, local copies, waits for them, and re-layouts: none -> 4.44 us  [the longest x4 2.21 us: waves_cut(): lax.dynamic_update_slice_in_dim(plain, view_out, (reached - ii) % block_n...]
    unnamed x46 -> x44, local copies, waits for them, and re-layouts: 11.2 us -> 12.2 us
  transfers between devices with their start and end apart: 3 -> 9, of which waited for: 3 -> 8; matrix products, arithmetic and copies ran while one was open for 8% -> 12% of each run, Pallas kernels for 0% -> 0%
where the time goes in v1:
time: 240 us; the launch traced here: 239 us
  waiting for transfers between devices  158 us (66%)
  local copies, waits for them, and re-layouts  23.5 us (10%)
  starting transfers between devices  19.8 us (8%)
  between operations  17.2 us (7%)
  other arithmetic  12.6 us (5%)
  matrix products  8.03 us (3%)
    ppermute x4, waiting for transfers between devices, waves_cut(): view_out = lax.ppermute(view_out, axis_name=device_axis, perm=row_list)  105 us
    reduce_scatter x1, waiting for transfers between devices, shards(): lax.psum_scatter(projected.astype(jnp.bfloat16), 'grp', scatter_dimension...  22.2 us
    all_gather x1, waiting for transfers between devices, shards(): lax.all_gather(upper_values, 'tok', axis=1, tiled=True)  17.3 us
    ppermute x3, waiting for transfers between devices, waves_cut(): vec_out = lax.ppermute(vec_out, axis_name=device_axis, perm=items)  13.8 us
    unnamed x44, local copies, waits for them, and re-layouts  12.2 us
    ppermute x4, starting transfers between devices, waves_cut(): view_out = lax.ppermute(view_out, axis_name=device_axis, perm=row_list)  10.4 us
    ppermute x3, starting transfers between devices, waves_cut(): vec_out = lax.ppermute(vec_out, axis_name=device_axis, perm=items)  9.28 us
  transfers between devices with their start and end apart: 9, of which 8 were waited for; matrix products, arithmetic and copies ran while one was open for 12% of the time, Pallas kernels for 0%

profile of v1, /device:TPU:0, one launch (start us, length us, event | category | flops | bytes accessed | tf_op | source)
XLA Modules:
  0.0 239.0 jit_solution(7620667656248120337)
XLA Ops:
  6.5 2.4 %copy.32 = bf16[6,128,512]{1,2,0:T(8,128)(2,1)} copy(bf16[6,128,512]{2,1,0:T(8,128)(2,1)} %param.22) | data formatting | bytes 1572864 | tf_op args[8]
  9.1 1.5 copy.27
  10.6 3.0 %collective-permute-start = (bf16[6,128,512]{1,2,0:T(8,128)(2,1)S(1)}, bf16[6,128,512]{1,2,0:T(8,128)(2,1)}, u32[]{:S(2)}, u32[]{:S(2)}) collective-permute-start(bf16[6,128,512]{1,2,0:T(8,128)(2,1)S(1)} %copy.27), channel_id=1, source_target_pairs={{0,4},{4,8},{8,12},{12,16},{16,20},{20,24},{24,28},{28,0},{1,5},{5... | collective-permute-start | bytes 2359304 | tf_op jit(solution)/shard_map/ppermute | solution.py:27
  13.6 3.1 %collective-permute-start.1 = (bf16[6,128,512]{1,2,0:T(8,128)(2,1)S(1)}, bf16[6,128,512]{1,2,0:T(8,128)(2,1)}, u32[]{:S(2)}, u32[]{:S(2)}) collective-permute-start(bf16[6,128,512]{1,2,0:T(8,128)(2,1)S(1)} %copy.27), channel_id=1, source_target_pairs={{0,28},{4,0},{8,4},{12,8},{16,12},{20,16},{24,20},{28,24},{1,29},{... | collective-permute-start | bytes 2359304 | tf_op jit(solution)/shard_map/ppermute | solution.py:32
  23.8 2.1 copy.24
  25.9 2.0 copy.25
  29.3 1.4 fusion.92
  33.3 22.3 %collective-permute-done = bf16[6,128,512]{1,2,0:T(8,128)(2,1)} collective-permute-done((bf16[6,128,512]{1,2,0:T(8,128)(2,1)S(1)}, bf16[6,128,512]{1,2,0:T(8,128)(2,1)}, u32[]{:S(2)}, u32[]{:S(2)}) %collective-permute-start) | collective-permute-done | bytes 786464 | tf_op jit(solution)/shard_map/ppermute | solution.py:27
  55.7 2.6 %collective-permute-start.2 = (bf16[6,128,512]{1,2,0:T(8,128)(2,1)}, bf16[6,128,512]{1,2,0:T(8,128)(2,1)S(1)}, u32[]{:S(2)}, u32[]{:S(2)}) collective-permute-start(bf16[6,128,512]{1,2,0:T(8,128)(2,1)} %collective-permute-done), channel_id=1, source_target_pairs={{0,4},{4,8},{8,12},{12,16},{16,20},{20,24},{24,28},{28,0},{1,5},{5... | collective-permute-start | bytes 2359304 | tf_op jit(solution)/shard_map/ppermute | solution.py:27
  59.3 3.1 %collective-permute-start.3 = (bf16[6,128,512]{1,2,0:T(8,128)(2,1)}, bf16[6,128,512]{1,2,0:T(8,128)(2,1)S(1)}, u32[]{:S(2)}, u32[]{:S(2)}) collective-permute-start(bf16[6,128,512]{1,2,0:T(8,128)(2,1)} %collective-permute-done.1), channel_id=1, source_target_pairs={{0,28},{4,0},{8,4},{12,8},{16,12},{20,16},{24,20},{28,24},{1,29},{... | collective-permute-start | bytes 2359304 | tf_op jit(solution)/shard_map/ppermute | solution.py:32
  63.1 33.5 %collective-permute-done.2 = bf16[6,128,512]{1,2,0:T(8,128)(2,1)S(1)} collective-permute-done((bf16[6,128,512]{1,2,0:T(8,128)(2,1)}, bf16[6,128,512]{1,2,0:T(8,128)(2,1)S(1)}, u32[]{:S(2)}, u32[]{:S(2)}) %collective-permute-start.2) | collective-permute-done | bytes 786464 | tf_op jit(solution)/shard_map/ppermute | solution.py:27
  96.5 2.4 collective-permute-start.4
  99.6 1.7 fusion
  102.7 3.1 %collective-permute-start.5 = (bf16[6,128,512]{1,2,0:T(8,128)(2,1)S(1)}, bf16[6,128,512]{1,2,0:T(8,128)(2,1)S(1)}, u32[]{:S(2)}, u32[]{:S(2)}) collective-permute-start(bf16[6,128,512]{1,2,0:T(8,128)(2,1)S(1)} %collective-permute-done.3), channel_id=1, source_target_pairs={{0,28},{4,0},{8,4},{12,8},{16,12},{20,16},{24,20},{28,24},{1,29},{... | collective-permute-start | bytes 2359304 | tf_op jit(solution)/shard_map/ppermute | solution.py:32
  106.9 41.7 %collective-permute-done.4 = bf16[6,128,512]{1,2,0:T(8,128)(2,1)S(1)} collective-permute-done((bf16[6,128,512]{1,2,0:T(8,128)(2,1)S(1)}, bf16[6,128,512]{1,2,0:T(8,128)(2,1)S(1)}, u32[]{:S(2)}, u32[]{:S(2)}) %collective-permute-start.4) | collective-permute-done | bytes 786464 | tf_op jit(solution)/shard_map/ppermute | solution.py:27
  148.6 2.5 %collective-permute-start.6 = (bf16[6,128,512]{1,2,0:T(8,128)(2,1)S(1)}, bf16[6,128,512]{1,2,0:T(8,128)(2,1)S(1)}, u32[]{:S(2)}, u32[]{:S(2)}) collective-permute-start(bf16[6,128,512]{1,2,0:T(8,128)(2,1)S(1)} %collective-permute-done.4), channel_id=1, source_target_pairs={{0,4},{4,8},{8,12},{12,16},{16,20},{20,24},{24,28},{28,0},{1,5},{5... | collective-permute-start | bytes 2359304 | tf_op jit(solution)/shard_map/ppermute | solution.py:27
  152.5 1.4 constant_dynamic-update-slice_fusion.5
  154.8 13.4 %collective-permute-done.5 = bf16[6,128,512]{1,2,0:T(8,128)(2,1)S(1)} collective-permute-done((bf16[6,128,512]{1,2,0:T(8,128)(2,1)S(1)}, bf16[6,128,512]{1,2,0:T(8,128)(2,1)S(1)}, u32[]{:S(2)}, u32[]{:S(2)}) %collective-permute-start.5) | collective-permute-done | bytes 786464 | tf_op jit(solution)/shard_map/ppermute | solution.py:32
  168.5 7.0 %collective-permute-done.6 = bf16[6,128,512]{1,2,0:T(8,128)(2,1)S(1)} collective-permute-done((bf16[6,128,512]{1,2,0:T(8,128)(2,1)S(1)}, bf16[6,128,512]{1,2,0:T(8,128)(2,1)S(1)}, u32[]{:S(2)}, u32[]{:S(2)}) %collective-permute-start.6) | collective-permute-done | bytes 786464 | tf_op jit(solution)/shard_map/ppermute | solution.py:27
  181.8 17.3 %all-gather.2.cloned.1.call-done = bf16[6,1024,512]{1,2,0:T(8,128)(2,1)} async-done(((bf16[6,128,512]{1,2,0:T(8,128)(2,1)}), bf16[6,1024,512]{1,2,0:T(8,128)(2,1)}) %all-gather.2.cloned.1.call-update) | async-done | bytes 6291472 | tf_op jit(solution)/shard_map/all_gather | solution.py:142
  199.1 1.8 constant_dynamic-slice_fusion.4
  206.8 1.5 convolution_convert_fusion
  208.3 22.2 %reduce-scatter.2.cloned.1.call-done = bf16[192,512]{1,0:T(8,128)(2,1)} async-done(((bf16[192,2048]{1,0:T(8,128)(2,1)}), bf16[192,512]{1,0:T(8,128)(2,1)}) %reduce-scatter.2.cloned.1.call-update) | async-done | bytes 196624 | tf_op jit(solution)/shard_map/reduce_scatter | solution.py:158
  230.5 1.7 add_convert_fusion
  (86 shorter events, 27.0 us)
Async XLA Ops:
  6.5 200.2 %copy-start = (bf16[512,2048]{1,0:T(8,128)(2,1)S(1)}, bf16[512,2048]{1,0:T(8,128)(2,1)}, u32[]{:S(2)}) copy-start(bf16[512,2048]{1,0:T(8,128)(2,1)} %param.18) | copy-start | bytes 6291460
  6.5 192.5 %all-gather.2.cloned.1.call-start = ((), (), s32[]{:S(2)}) async-start(), calls=%async_computation.1 | async-start | bytes 7077888 | tf_op jit(solution)/shard_map/all_gather | solution.py:142
  9.0 7.7 %copy-start.15 = (s32[8]{0:T(128)S(1)}, s32[8]{0:T(128)}, u32[]{:S(2)}) copy-start(s32[8]{0:T(128)} %param.24) | copy-start | bytes 100
  9.0 7.7 %copy-start.16 = (s32[8]{0:T(128)S(1)}, s32[8]{0:T(128)}, u32[]{:S(2)}) copy-start(s32[8]{0:T(128)} %param.27) | copy-start | bytes 100
  9.0 9.7 %copy-start.18 = (s32[4]{0:T(128)S(1)}, s32[4]{0:T(128)}, u32[]{:S(2)}) copy-start(s32[4]{0:T(128)} %param.25) | copy-start | bytes 52
  9.0 221.5 %reduce-scatter.2.cloned.1.call-start = ((), (), s32[]{:S(2)}) async-start(), calls=%async_computation.2 | async-start | bytes 983040 | tf_op jit(solution)/shard_map/reduce_scatter | solution.py:158
  10.6 45.1 %collective-permute-start = (bf16[6,128,512]{1,2,0:T(8,128)(2,1)S(1)}, bf16[6,128,512]{1,2,0:T(8,128)(2,1)}, u32[]{:S(2)}, u32[]{:S(2)}) collective-permute-start(bf16[6,128,512]{1,2,0:T(8,128)(2,1)S(1)} %copy.27), channel_id=1, source_target_pairs={{0,4},{4,8},{8,12},{12,16},{16,20},{20,24},{24,28},{28,0},{1,5},{5... | collective-permute-start | bytes 2359304 | tf_op jit(solution)/shard_map/ppermute | solution.py:27
  13.6 45.7 %collective-permute-start.1 = (bf16[6,128,512]{1,2,0:T(8,128)(2,1)S(1)}, bf16[6,128,512]{1,2,0:T(8,128)(2,1)}, u32[]{:S(2)}, u32[]{:S(2)}) collective-permute-start(bf16[6,128,512]{1,2,0:T(8,128)(2,1)S(1)} %copy.27), channel_id=1, source_target_pairs={{0,28},{4,0},{8,4},{12,8},{16,12},{20,16},{24,20},{28,24},{1,29},{... | collective-permute-start | bytes 2359304 | tf_op jit(solution)/shard_map/ppermute | solution.py:32
  22.7 6.5 %copy-start.17 = (s32[6]{0:T(128)S(1)}, s32[6]{0:T(128)}, u32[]{:S(2)}) copy-start(s32[6]{0:T(128)} %param.26) | copy-start | bytes 76
  22.7 8.6 %copy-start.19 = (s32[8]{0:T(128)S(1)}, s32[8]{0:T(128)}, u32[]{:S(2)}) copy-start(s32[8]{0:T(128)} %param.23) | copy-start | bytes 100
  23.8 34.5 %copy-start.13 = (bf16[192,512]{1,0:T(8,128)(2,1)S(1)}, bf16[192,512]{1,0:T(8,128)(2,1)}, u32[]{:S(2)}) copy-start(bf16[192,512]{1,0:T(8,128)(2,1)} %param.15) | copy-start | bytes 589828
  23.8 75.8 %copy-start.9 = (bf16[192,512]{1,0:T(8,128)(2,1)S(1)}, bf16[192,512]{1,0:T(8,128)(2,1)}, u32[]{:S(2)}) copy-start(bf16[192,512]{1,0:T(8,128)(2,1)} %param.14) | copy-start | bytes 589828
  55.7 40.9 %collective-permute-start.2 = (bf16[6,128,512]{1,2,0:T(8,128)(2,1)}, bf16[6,128,512]{1,2,0:T(8,128)(2,1)S(1)}, u32[]{:S(2)}, u32[]{:S(2)}) collective-permute-start(bf16[6,128,512]{1,2,0:T(8,128)(2,1)} %collective-permute-done), channel_id=1, source_target_pairs={{0,4},{4,8},{8,12},{12,16},{16,20},{20,24},{24,28},{28,0},{1,5},{5... | collective-permute-start | bytes 2359304 | tf_op jit(solution)/shard_map/ppermute | solution.py:27
  59.3 43.2 %collective-permute-start.3 = (bf16[6,128,512]{1,2,0:T(8,128)(2,1)}, bf16[6,128,512]{1,2,0:T(8,128)(2,1)S(1)}, u32[]{:S(2)}, u32[]{:S(2)}) collective-permute-start(bf16[6,128,512]{1,2,0:T(8,128)(2,1)} %collective-permute-done.1), channel_id=1, source_target_pairs={{0,28},{4,0},{8,4},{12,8},{16,12},{20,16},{24,20},{28,24},{1,29},{... | collective-permute-start | bytes 2359304 | tf_op jit(solution)/shard_map/ppermute | solution.py:32
  96.5 52.1 %collective-permute-start.4 = (bf16[6,128,512]{1,2,0:T(8,128)(2,1)S(1)}, bf16[6,128,512]{1,2,0:T(8,128)(2,1)S(1)}, u32[]{:S(2)}, u32[]{:S(2)}) collective-permute-start(bf16[6,128,512]{1,2,0:T(8,128)(2,1)S(1)} %collective-permute-done.2), channel_id=1, source_target_pairs={{0,4},{4,8},{8,12},{12,16},{16,20},{20,24},{24,28},{28,0},{1,5},{5... | collective-permute-start | bytes 2359304 | tf_op jit(solution)/shard_map/ppermute | solution.py:27
  101.3 1.4 copy-start.10
  102.7 65.4 %collective-permute-start.5 = (bf16[6,128,512]{1,2,0:T(8,128)(2,1)S(1)}, bf16[6,128,512]{1,2,0:T(8,128)(2,1)S(1)}, u32[]{:S(2)}, u32[]{:S(2)}) collective-permute-start(bf16[6,128,512]{1,2,0:T(8,128)(2,1)S(1)} %collective-permute-done.3), channel_id=1, source_target_pairs={{0,28},{4,0},{8,4},{12,8},{16,12},{20,16},{24,20},{28,24},{1,29},{... | collective-permute-start | bytes 2359304 | tf_op jit(solution)/shard_map/ppermute | solution.py:32
  148.6 26.8 %collective-permute-start.6 = (bf16[6,128,512]{1,2,0:T(8,128)(2,1)S(1)}, bf16[6,128,512]{1,2,0:T(8,128)(2,1)S(1)}, u32[]{:S(2)}, u32[]{:S(2)}) collective-permute-start(bf16[6,128,512]{1,2,0:T(8,128)(2,1)S(1)} %collective-permute-done.4), channel_id=1, source_target_pairs={{0,4},{4,8},{8,12},{12,16},{16,20},{20,24},{24,28},{28,0},{1,5},{5... | collective-permute-start | bytes 2359304 | tf_op jit(solution)/shard_map/ppermute | solution.py:27
  199.1 2.0 copy-start.6
  200.8 1.5 copy-start.8
  201.1 1.7 copy-start.12
  201.6 1.8 copy-start.11
  203.4 1.4 copy-start.2
  206.7 23.8 %copy-start.14 = (bf16[192,512]{1,0:T(8,128)(2,1)S(1)}, bf16[192,512]{1,0:T(8,128)(2,1)}, u32[]{:S(2)}) copy-start(bf16[192,512]{1,0:T(8,128)(2,1)} %param.17) | copy-start | bytes 589828
  (5 other events, 6.2 us)
Sparse Core Ops, SparseCore 0:
  9.4 189.6 all-gather.1
  208.4 22.0 reduce-scatter.1
